TPU v7x, 256 devices: a whole 4x4x8 slice. The times are simulated.
256 devices in a mesh: req: 64 (over y_lo, z, x), tp: 4 (over y_hi, core).
Axes of the slice: x: 4, y: 4 (y_hi: 2, y_lo: 2; y = y_hi * 2 + y_lo), z: 8, core: 2. Of those that a mesh axis runs over, the one named last changes fastest.
Arguments:
- query_heads: bfloat16 [61440, 4096], P('req', 'tp'), parts along dimension 0, may hold values from -140 to 140
- normed_key_heads: bfloat16 [61440, 512], P('req', 'tp'), parts along dimension 0, may hold values from -7 to 7
- value_rows_per_head: bfloat16 [61440, 512], P('req', 'tp'), parts along dimension 0, may hold values from -6 to 6
- residual_in: bfloat16 [61440, 2048], P(('req', 'tp')), parts along dimension 0, may hold values from -6 to 6
- out_weight: bfloat16 [4096, 2048], P('tp'), may hold values from -0.09375 to 0.09375
- norm_gain: float32 [2048], replicated, may hold values from 0.3 to 3
- gate_up: bfloat16 [2, 2, 2048, 768], P(None, None, None, 'tp'), may hold values from -0.125 to 0.125
- down_weight: bfloat16 [2, 768, 2048], P(None, 'tp'), may hold values from -0.21875 to 0.21875
- segment_ids: int32 [61440], P('req'), parts along dimension 0, may hold values from 0 to 5, never falling along the last dimension, each value on 1 to 480 neighbouring positions
- expert_ids: int32 [61440, 8], P('req'), parts along dimension 0, may hold values from 0 to 127, all different within a row; in each aligned block of 960 rows (0 to 959, 960 to 1919, ...) at most 75 rows name the same one
- gate_weights: float32 [61440, 8], P('req'), parts along dimension 0, may hold values from 0.05 to 0.8
Outputs:
- layer_out: bfloat16 [61440, 2048], P(('req', 'tp')), parts along dimension 0
There are 64 independent parts, one for each index of `req`. A program takes and returns all parts, laid end to end along the dimension named above; an argument that names none is the same for every part. Nothing has to cross between parts.
Inputs may be any that keep to these rules, and one draw needn't show every extreme that they name: `segment_ids`: segment ids never fall along the tokens; each prompt has 1 to 480 tokens and one has exactly 480. `expert_ids`: the 8 experts of a token are distinct; no expert is chosen by more than 75 tokens of a request group, a bound that some block reaches.
All inputs are finite; a program needn't handle non-finite values.
Results may differ from a plain program's by a relative error of at most 0.0053.
Values may be sent and summed in bfloat16 or wider, within the bound.
No kernel may reach another device: no remote copies, remote signals or barrier semaphores. Data moves between devices by JAX's collectives and lax.ppermute only.
A program may use at most 128 MiB of HBM per device.

v0:
```python
import math
import jax
import jax.numpy as jnp
from jax import lax
from jax.sharding import PartitionSpec as P

QUERY_HEADS = 32
KEY_VALUE_HEADS = 4
HEAD_WIDTH = 128
EXPERTS = 128


def positions_of(segment_ids):
    earlier = (segment_ids[None, :] < segment_ids[:, None]).astype(jnp.int32)
    return jnp.arange(segment_ids.shape[0], dtype=jnp.int32) - jnp.sum(earlier, axis=1)


def rotary_tables(vectors, token_positions):
    half_dim = vectors.shape[-1] // 2
    frequency = 1000000.0 ** (-jnp.arange(half_dim, dtype=jnp.float32) / half_dim)
    angles = token_positions.astype(jnp.float32)[:, None] * frequency[None, :]
    cosine = jnp.cos(angles)[:, None, :]
    sine = jnp.sin(angles)[:, None, :]
    first = vectors[..., :half_dim]
    second = vectors[..., half_dim:]
    return jnp.concatenate(
        [first * cosine - second * sine, second * cosine + first * sine], axis=-1
    )


def rms_norm(hidden, gain):
    widened = hidden.astype(jnp.float32)
    factor = lax.rsqrt(jnp.mean(widened * widened, axis=-1, keepdims=True) + 1e-06)
    return (widened * factor * gain).astype(jnp.bfloat16)


def compact(chosen, limit):
    total = chosen.shape[0]
    iota = jnp.arange(total, dtype=jnp.int32)
    ranked = jnp.where(chosen, iota, iota + total)
    order = jnp.argsort(ranked, stable=True)[:limit]
    return (order, chosen[order])


def attend(query_heads, normed_key_heads, value_rows_per_head, segment_ids):
    item_count = segment_ids.shape[0]
    token_positions = positions_of(segment_ids)
    kv_local = normed_key_heads.shape[1] // HEAD_WIDTH
    query_group_width = QUERY_HEADS // KEY_VALUE_HEADS
    queries = rotary_tables(
        query_heads.reshape(item_count, kv_local * query_group_width, HEAD_WIDTH).astype(
            jnp.float32
        ),
        token_positions,
    ).astype(jnp.bfloat16)
    keys_after_rotary = rotary_tables(
        normed_key_heads.reshape(item_count, kv_local, HEAD_WIDTH).astype(jnp.float32),
        token_positions,
    ).astype(jnp.bfloat16)
    values = value_rows_per_head.reshape(item_count, kv_local, HEAD_WIDTH)
    indices = jnp.arange(item_count)
    allowed = (segment_ids[:, None] == segment_ids[None, :]) & (
        indices[None, :] <= indices[:, None]
    )
    factor = 1.0 / math.sqrt(HEAD_WIDTH)
    key_one = keys_after_rotary[:, 0]
    value_one = values[:, 0]

    def one_head(query_one, key_one=key_one, value_one=value_one):
        scores = jnp.dot(query_one, key_one.T, preferred_element_type=jnp.float32) * factor
        scores = jnp.where(allowed, scores, -1e30)
        peak = jnp.max(scores, axis=1, keepdims=True)
        weights = jnp.exp(scores - peak)
        weights = (weights / jnp.sum(weights, axis=1, keepdims=True)).astype(jnp.bfloat16)
        return jnp.dot(weights, value_one, preferred_element_type=jnp.float32).astype(jnp.bfloat16)

    group_queries = queries.transpose(1, 0, 2)
    blocks = lax.map(one_head, group_queries)
    attended = blocks.transpose(1, 0, 2)
    return attended.reshape(item_count, kv_local * query_group_width * HEAD_WIDTH)


def local(
    query_heads,
    normed_key_heads,
    value_rows_per_head,
    residual_in,
    out_weight,
    norm_gain,
    gate_up,
    down_weight,
    segment_ids,
    expert_ids,
    gate_weights,
):
    attended = attend(query_heads, normed_key_heads, value_rows_per_head, segment_ids)
    tok_rows = residual_in.shape[0]
    width = residual_in.shape[1]
    group_tokens = expert_ids.shape[0]
    capacity = group_tokens * expert_ids.shape[1] * 5 // (EXPERTS * 4)
    window = gate_up.shape[0]
    slots = jnp.arange(window, dtype=jnp.int32)
    route_all = jnp.sum(
        jnp.where(expert_ids[:, :, None] == slots[None, None, :], gate_weights[:, :, None], 0.0),
        axis=1,
    )
    normed_all = None
    rows = attended
    projected = lax.psum_scatter(
        jnp.dot(rows, out_weight, preferred_element_type=jnp.float32),
        "tp",
        scatter_dimension=0,
        tiled=True,
    )
    mixed = (residual_in.astype(jnp.float32) + projected).astype(jnp.bfloat16)
    normed = rms_norm(mixed, norm_gain)
    normed_all = lax.all_gather(normed, "tp", axis=0, tiled=True)
    rows = normed_all
    limit = min(capacity, tok_rows * lax.axis_size("tp"))
    summed = jnp.zeros((tok_rows * lax.axis_size("tp"), width), jnp.float32)
    for expert in range(window):
        taken, valid = compact(jnp.any(expert_ids == expert, axis=1), limit)
        picked = rows[taken]
        gate = jnp.dot(picked, gate_up[expert, 0], preferred_element_type=jnp.float32)
        upward = jnp.dot(picked, gate_up[expert, 1], preferred_element_type=jnp.float32)
        active = (jax.nn.silu(gate) * upward).astype(jnp.bfloat16)
        outputs = jnp.dot(active, down_weight[expert], preferred_element_type=jnp.float32)
        scale = jnp.where(valid, route_all[taken, expert], 0.0)
        summed = summed.at[taken].add(scale[:, None] * outputs)
    experts = lax.psum_scatter(summed, "tp", scatter_dimension=0, tiled=True)
    return (mixed.astype(jnp.float32) + experts).astype(jnp.bfloat16)


def solution(mesh):
    placed = (
        P("req", "tp"),
        P("req", "tp"),
        P("req", "tp"),
        P(("req", "tp"), None),
        P("tp", None),
        P(),
        P(None, None, None, "tp"),
        P(None, "tp", None),
        P("req"),
        P("req", None),
        P("req", None),
    )
    return jax.shard_map(
        local, mesh=mesh, in_specs=placed, out_specs=P(("req", "tp"), None), check_vma=False
    )
```

profile of v0, /device:TPU:1, one launch (start us, length us, event | category | flops | bytes accessed | tf_op | source)
XLA Modules:
  0.0 299.4 jit_solution(11987907407622865133)
XLA Ops:
  9.0 1.8 multiply_cosine_fusion.1
  10.7 2.3 fusion.49
  18.0 25.1 %while.11 = (s32[]{:T(128)}, bf16[8,960,128]{2,1,0:T(8,128)(2,1)}, bf16[8,960,128]{2,1,0:T(8,128)(2,1)S(1)}, bf16[960,128]{1,0:T(8,128)(2,1)S(1)}, bf16[960,128]...) while((s32[]{:T(128)}, bf16[8,960,128]{2,1,0:T(8,128)(2,1)}, ...), condition=%wide.region_4.5_spmd.clone, body=%wide.region_1.4_spmd.clone.sunk | while | flops 482117760 | bytes 12069725 | solution.py:78
  25.8 1.6 fusion.83
  29.0 1.6 fusion.83
  32.1 1.6 fusion.83
  35.3 1.6 fusion.83
  38.4 1.6 fusion.83
  43.1 10.1 %fusion.17 = f32[960,2048]{1,0:T(8,128)} fusion(bf16[1024,2048]{1,0:T(8,128)(2,1)} %param.17, bf16[8,960,128]{2,1,0:T(8,128)(2,1)} %get-tuple-element.39), kind=kOutput, calls=%fused_computation.37 | convolution fusion | flops 4026531840 | bytes 14024704 | tf_op jit(solution)/shard_map/dot_general | solution.py:110
  53.5 85.1 %reduce-scatter.3.cloned.1.call-done = f32[240,2048]{1,0:T(8,128)} async-done(((f32[960,2048]{1,0:T(8,128)}), f32[240,2048]{1,0:T(8,128)}) %reduce-scatter.3.cloned.1.call-update) | async-done | bytes 1966096 | tf_op jit(solution)/shard_map/reduce_scatter | solution.py:109
  138.6 1.9 fusion.13
  141.9 4.4 %sort.32 = (s32[960]{0:T(1024)}, s32[960]{0:T(1024)S(1)}) sort(s32[960]{0:T(1024)S(1)} %get-tuple-element.103, s32[960]{0:T(1024)S(1)} %iota.47), dimensions={0}, to_apply=%region_12.13 | sort | flops 9600 | bytes 15360 | tf_op jit(solution)/shard_map/jit(argsort)/sort | solution.py:41
  147.6 2.0 gather_fusion.4
  149.7 4.4 %sort.31 = (s32[960]{0:T(1024)}, s32[960]{0:T(1024)S(1)}) sort(s32[960]{0:T(1024)S(1)} %get-tuple-element.104, s32[960]{0:T(1024)S(1)} %iota.45), dimensions={0}, to_apply=%region_7.8 | sort | flops 9600 | bytes 15360 | tf_op jit(solution)/shard_map/jit(argsort)/sort | solution.py:41
  154.0 2.0 gather_fusion.1
  157.4 24.6 %all-gather.2.cloned.1.call-done = bf16[960,2048]{1,0:T(8,128)(2,1)} async-done(((bf16[240,2048]{1,0:T(8,128)(2,1)}), bf16[960,2048]{1,0:T(8,128)(2,1)}) %all-gather.2.cloned.1.call-update) | async-done | bytes 3932176 | tf_op jit(solution)/shard_map/all_gather | solution.py:117
  182.0 3.7 %gather_fusion.2 = bf16[75,2048]{1,0:T(8,128)(2,1)S(1)} fusion(bf16[960,2048]{1,0:T(8,128)(2,1)} %all-gather.2.cloned.1.call-done, s32[1024]{0:T(1024)S(1)} %pad_clamp_fusion.1), kind=kCustom, calls=%fused_computation.2 | custom fusion | bytes 614700 | tf_op jit(solution)/shard_map/gather | solution.py:123
  187.2 3.7 %gather_fusion.5 = bf16[75,2048]{1,0:T(8,128)(2,1)S(1)} fusion(bf16[960,2048]{1,0:T(8,128)(2,1)} %all-gather.2.cloned.1.call-done, s32[1024]{0:T(1024)S(1)} %pad_clamp_fusion), kind=kCustom, calls=%fused_computation.5 | custom fusion | bytes 614700 | tf_op jit(solution)/shard_map/gather | solution.py:123
  192.4 2.1 convolution_multiply_fusion
  194.6 2.1 convolution_multiply_fusion.1
  196.7 5.0 %scatter_custom_fusion = f32[960,2048]{1,0:T(8,128)} fusion(s32[75]{0:T(128)S(1)} %get-tuple-element.92, f32[75,2048]{1,0:T(8,128)S(1)} %convolution_multiply_fusion.1, f32[]{:T(128)} %constant.16.clone.1), kind=kCustom, calls=%fused_computation.23 | custom fusion | flops 153600 | bytes 7864324 | tf_op jit(solution)/shard_map/scatter-add | solution.py:129
  201.8 7.8 %scatter_fusion = f32[960,2048]{1,0:T(8,128)} fusion(f32[960,2048]{1,0:T(8,128)} %scatter_custom_fusion, s32[75]{0:T(128)S(1)} %get-tuple-element.90, f32[75,2048]{1,0:T(8,128)S(1)} %convolution_multiply_fusion), kind=kCustom, calls=%fused_computation.7 | custom fusion | flops 153600 | bytes 1843500 | tf_op jit(solution)/shard_map/scatter-add | solution.py:129
  209.6 80.6 %reduce-scatter.5.cloned.1.call-done = f32[240,2048]{1,0:T(8,128)} async-done(((f32[960,2048]{1,0:T(8,128)}), f32[240,2048]{1,0:T(8,128)}) %reduce-scatter.5.cloned.1.call-update) | async-done | bytes 1966096 | tf_op jit(solution)/shard_map/reduce_scatter | solution.py:130
  290.1 2.7 fusion.16
  (67 shorter events, 31.8 us)
Async XLA Ops:
  6.5 6.5 %copy-start = (bf16[960,1024]{1,0:T(8,128)(2,1)S(1)}, bf16[960,1024]{1,0:T(8,128)(2,1)}, u32[]{:S(2)}) copy-start(bf16[960,1024]{1,0:T(8,128)(2,1)} %param.13) | copy-start | bytes 5898244
  6.5 132.1 %reduce-scatter.3.cloned.1.call-start = ((), (), s32[]{:S(2)}) async-start(), calls=%async_computation.2 | async-start | bytes 9830400 | tf_op jit(solution)/shard_map/reduce_scatter | solution.py:109
  17.0 0.7 copy-start.4
  17.0 1.0 copy-start.6
  53.2 85.4 %copy-start.1 = (bf16[240,2048]{1,0:T(8,128)(2,1)S(1)}, bf16[240,2048]{1,0:T(8,128)(2,1)}, u32[]{:S(2)}) copy-start(bf16[240,2048]{1,0:T(8,128)(2,1)} %param.16) | copy-start | bytes 2949124
  53.2 87.3 %copy-start.5 = (f32[2048]{0:T(1024)S(1)}, f32[2048]{0:T(1024)}, u32[]{:S(2)}) copy-start(f32[2048]{0:T(1024)} %param.18) | copy-start | bytes 24580
  53.2 88.6 %copy-start.2 = (s32[960,8]{0,1:T(8,128)S(1)}, s32[960,8]{0,1:T(8,128)}, u32[]{:S(2)}) copy-start(s32[960,8]{0,1:T(8,128)} %param.22) | copy-start | bytes 92164
  53.3 94.3 %copy-start.3 = (f32[960,8]{0,1:T(8,128)S(1)}, f32[960,8]{0,1:T(8,128)}, u32[]{:S(2)}) copy-start(f32[960,8]{0,1:T(8,128)} %param.23) | copy-start | bytes 92164
  53.3 128.8 %all-gather.2.cloned.1.call-start = ((), (), s32[]{:S(2)}) async-start(), calls=%async_computation.3 | async-start | bytes 4915200 | tf_op jit(solution)/shard_map/all_gather | solution.py:117
  141.8 148.3 %reduce-scatter.5.cloned.1.call-start = ((), (), s32[]{:S(2)}) async-start(), calls=%async_computation.4 | async-start | bytes 9830400 | tf_op jit(solution)/shard_map/reduce_scatter | solution.py:130
Sparse Core Ops, SparseCore 0:
  53.4 85.1 reduce-scatter.2
  141.9 40.0 all-gather.1
  209.7 80.3 reduce-scatter.4
where the time goes:
time: 300 us; the launch traced here: 299 us
  waiting for transfers between devices  190 us (63%)
  other arithmetic  41.9 us (14%)
  matrix products  37.7 us (13%)
  local copies, waits for them, and re-layouts  15.8 us (5%)
  between operations  13.4 us (4%)
    reduce_scatter x1, waiting for transfers between devices, local(): lax.psum_scatter(jnp.dot(rows, out_weight, preferred_element_type=jnp.flo...  85.1 us
    reduce_scatter x1, waiting for transfers between devices, local(): experts = lax.psum_scatter(summed, 'tp', scatter_dimension=0, tiled=True)  80.6 us
    all_gather x1, waiting for transfers between devices, local(): normed_all = lax.all_gather(normed, 'tp', axis=0, tiled=True)  24.6 us
    scatter-add x2, other arithmetic, local(): summed = summed.at[taken].add(scale[:, None] * outputs)  12.8 us
    dot_general x8, matrix products, one_head(): jnp.dot(weights, value_one, preferred_element_type=jnp.float32)  12.4 us
    dot_general x1, matrix products, local(): jnp.dot(rows, out_weight, preferred_element_type=jnp.float32)  10.1 us
    sort x2, other arithmetic, compact(): order = jnp.argsort(ranked, stable=True)[:limit]  8.71 us
    dot_general x8, matrix products, one_head(): jnp.dot(query_one, key_one.T, preferred_element_type=jnp.float32) * factor  7.91 us
  transfers between devices with their start and end apart: 3, of which 3 were waited for; matrix products, arithmetic and copies ran while one was open for 5% of the time, Pallas kernels for 0%

commit v1 on v0

--- a/solution.py
+++ b/solution.py
@@ -114,7 +114,9 @@
     )
     mixed = (residual_in.astype(jnp.float32) + projected).astype(jnp.bfloat16)
     normed = rms_norm(mixed, norm_gain)
-    normed_all = lax.all_gather(normed, "tp", axis=0, tiled=True)
+    normed_all = jnp.concatenate(
+        lax.all_to_all(jnp.stack([normed for _ in range(lax.axis_size("tp"))]), "tp", 0, 0), 0
+    )
     rows = normed_all
     limit = min(capacity, tok_rows * lax.axis_size("tp"))
     summed = jnp.zeros((tok_rows * lax.axis_size("tp"), width), jnp.float32)

time: 300 us -> 313 us (1.043)
  waiting for transfers between devices: 190 us -> 196 us
  starting transfers between devices: 0.27 us -> 5.73 us
    all_to_all x0 -> x1, waiting for transfers between devices: none -> 30.2 us  [local(): lax.all_to_all(jnp.stack([normed for _ in range(lax.axis_size('tp'))]), '...]
    all_gather x1 -> x0, waiting for transfers between devices: 24.6 us -> none  [local(): normed_all = lax.all_gather(normed, 'tp', axis=0, tiled=True)]
    all_to_all x0 -> x1, starting transfers between devices: none -> 5.73 us  [local(): lax.all_to_all(jnp.stack([normed for _ in range(lax.axis_size('tp'))]), '...]
where the time goes in v1:
time: 313 us
  waiting for transfers between devices  196 us (63%)
  other arithmetic  41.1 us (13%)
  matrix products  37.8 us (12%)
  local copies, waits for them, and re-layouts  18.4 us (6%)
  between operations  13.7 us (4%)
  starting transfers between devices  5.73 us (2%)
    reduce_scatter x1, waiting for transfers between devices, local(): lax.psum_scatter(jnp.dot(rows, out_weight, preferred_element_type=jnp.flo...  85.3 us
    reduce_scatter x1, waiting for transfers between devices, local(): experts = lax.psum_scatter(summed, 'tp', scatter_dimension=0, tiled=True)  80.7 us
    all_to_all x1, waiting for transfers between devices, local(): lax.all_to_all(jnp.stack([normed for _ in range(lax.axis_size('tp'))]), '...  30.2 us
    scatter-add x2, other arithmetic, local(): summed = summed.at[taken].add(scale[:, None] * outputs)  12.8 us
    dot_general x8, matrix products, one_head(): jnp.dot(weights, value_one, preferred_element_type=jnp.float32)  12.4 us
    dot_general x1, matrix products, local(): jnp.dot(rows, out_weight, preferred_element_type=jnp.float32)  10.1 us
    sort x2, other arithmetic, compact(): order = jnp.argsort(ranked, stable=True)[:limit]  8.74 us
    dot_general x8, matrix products, one_head(): jnp.dot(query_one, key_one.T, preferred_element_type=jnp.float32) * factor  7.93 us
  transfers between devices with their start and end apart: 3, of which 3 were waited for; matrix products, arithmetic and copies ran while one was open for 5% of the time, Pallas kernels for 0%

profile of v1, /device:TPU:1, one launch (start us, length us, event | category | flops | bytes accessed | tf_op | source)
XLA Modules:
  0.0 312.9 jit_solution(3286251207151563673)
XLA Ops:
  9.0 1.8 multiply_cosine_fusion.1
  10.7 2.5 fusion.49
  18.2 25.1 %while.11 = (s32[]{:T(128)}, bf16[8,960,128]{2,1,0:T(8,128)(2,1)}, bf16[8,960,128]{2,1,0:T(8,128)(2,1)S(1)}, bf16[960,128]{1,0:T(8,128)(2,1)S(1)}, bf16[960,128]...) while((s32[]{:T(128)}, bf16[8,960,128]{2,1,0:T(8,128)(2,1)}, ...), condition=%wide.region_4.5_spmd.clone, body=%wide.region_1.4_spmd.clone.sunk | while | flops 482117760 | bytes 12069725 | solution.py:78
  26.0 1.6 fusion.83
  29.2 1.6 fusion.83
  35.5 1.6 fusion.83
  43.3 10.1 %fusion.17 = f32[960,2048]{1,0:T(8,128)} fusion(bf16[1024,2048]{1,0:T(8,128)(2,1)} %param.17, bf16[8,960,128]{2,1,0:T(8,128)(2,1)} %get-tuple-element.39), kind=kOutput, calls=%fused_computation.37 | convolution fusion | flops 4026531840 | bytes 14024704 | tf_op jit(solution)/shard_map/dot_general | solution.py:110
  53.4 85.3 %reduce-scatter.3.cloned.1.call-done = f32[240,2048]{1,0:T(8,128)} async-done(((f32[960,2048]{1,0:T(8,128)}), f32[240,2048]{1,0:T(8,128)}) %reduce-scatter.3.cloned.1.call-update) | async-done | bytes 1966096 | tf_op jit(solution)/shard_map/reduce_scatter | solution.py:109
  138.8 1.9 fusion.13
  141.0 2.4 stack.2
  143.4 5.7 %all-to-all-start = ((bf16[4,240,2048]{2,1,0:T(8,128)(2,1)}), bf16[4,240,2048]{2,1,0:T(8,128)(2,1)}, u32[]{:S(2)}, u32[]{:S(2)}) async-start(bf16[4,240,2048]{2,1,0:T(8,128)(2,1)} %stack.2), calls=%async_computation.1 | async-start | bytes 7864320 | tf_op jit(solution)/shard_map/all_to_all | solution.py:118
  149.2 4.4 %sort.32 = (s32[960]{0:T(1024)}, s32[960]{0:T(1024)S(1)}) sort(s32[960]{0:T(1024)S(1)} %get-tuple-element.103, s32[960]{0:T(1024)S(1)} %iota.47), dimensions={0}, to_apply=%region_12.13 | sort | flops 9600 | bytes 15360 | tf_op jit(solution)/shard_map/jit(argsort)/sort | solution.py:41
  155.1 2.0 gather_fusion.4
  157.2 4.4 %sort.31 = (s32[960]{0:T(1024)}, s32[960]{0:T(1024)S(1)}) sort(s32[960]{0:T(1024)S(1)} %get-tuple-element.104, s32[960]{0:T(1024)S(1)} %iota.45), dimensions={0}, to_apply=%region_7.8 | sort | flops 9600 | bytes 15360 | tf_op jit(solution)/shard_map/jit(argsort)/sort | solution.py:41
  161.5 2.0 gather_fusion.1
  164.9 30.2 %all-to-all-done = bf16[4,240,2048]{2,1,0:T(8,128)(2,1)} async-done(((bf16[4,240,2048]{2,1,0:T(8,128)(2,1)}), bf16[4,240,2048]{2,1,0:T(8,128)(2,1)}, u32[]{:S(2)}, u32[]{:S(2)}) %all-to-all-start) | async-done | bytes 3932192 | tf_op jit(solution)/shard_map/all_to_all | solution.py:118
  195.1 3.7 %gather_fusion.5 = bf16[75,2048]{1,0:T(8,128)(2,1)S(1)} fusion(bf16[960,2048]{1,0:T(8,128)(2,1)} %bitcast.6, s32[1024]{0:T(1024)S(1)} %pad_clamp_fusion), kind=kCustom, calls=%fused_computation.5 | custom fusion | bytes 614700 | tf_op jit(solution)/shard_map/gather | solution.py:125
  198.8 3.7 %gather_fusion.2 = bf16[75,2048]{1,0:T(8,128)(2,1)S(1)} fusion(bf16[960,2048]{1,0:T(8,128)(2,1)} %bitcast.6, s32[1024]{0:T(1024)S(1)} %pad_clamp_fusion.1), kind=kCustom, calls=%fused_computation.2 | custom fusion | bytes 614700 | tf_op jit(solution)/shard_map/gather | solution.py:125
  205.5 2.1 convolution_multiply_fusion
  207.7 2.1 convolution_multiply_fusion.1
  209.8 5.0 %scatter_custom_fusion = f32[960,2048]{1,0:T(8,128)} fusion(s32[75]{0:T(128)S(1)} %get-tuple-element.92, f32[75,2048]{1,0:T(8,128)S(1)} %convolution_multiply_fusion.1, f32[]{:T(128)} %constant.16.clone.1), kind=kCustom, calls=%fused_computation.23 | custom fusion | flops 153600 | bytes 7864324 | tf_op jit(solution)/shard_map/scatter-add | solution.py:131
  214.8 7.8 %scatter_fusion = f32[960,2048]{1,0:T(8,128)} fusion(f32[960,2048]{1,0:T(8,128)} %scatter_custom_fusion, s32[75]{0:T(128)S(1)} %get-tuple-element.90, f32[75,2048]{1,0:T(8,128)S(1)} %convolution_multiply_fusion), kind=kCustom, calls=%fused_computation.7 | custom fusion | flops 153600 | bytes 1843500 | tf_op jit(solution)/shard_map/scatter-add | solution.py:131
  222.6 80.7 %reduce-scatter.5.cloned.1.call-done = f32[240,2048]{1,0:T(8,128)} async-done(((f32[960,2048]{1,0:T(8,128)}), f32[240,2048]{1,0:T(8,128)}) %reduce-scatter.5.cloned.1.call-update) | async-done | bytes 1966096 | tf_op jit(solution)/shard_map/reduce_scatter | solution.py:132
  303.3 2.7 fusion.16
  (67 shorter events, 33.9 us)
Async XLA Ops:
  6.5 6.7 %copy-start = (bf16[960,1024]{1,0:T(8,128)(2,1)S(1)}, bf16[960,1024]{1,0:T(8,128)(2,1)}, u32[]{:S(2)}) copy-start(bf16[960,1024]{1,0:T(8,128)(2,1)} %param.13) | copy-start | bytes 5898244
  6.5 132.2 %reduce-scatter.3.cloned.1.call-start = ((), (), s32[]{:S(2)}) async-start(), calls=%async_computation.3 | async-start | bytes 9830400 | tf_op jit(solution)/shard_map/reduce_scatter | solution.py:109
  17.2 0.7 copy-start.4
  17.2 1.0 copy-start.6
  53.4 85.4 %copy-start.1 = (bf16[240,2048]{1,0:T(8,128)(2,1)S(1)}, bf16[240,2048]{1,0:T(8,128)(2,1)}, u32[]{:S(2)}) copy-start(bf16[240,2048]{1,0:T(8,128)(2,1)} %param.16) | copy-start | bytes 2949124
  53.4 87.3 %copy-start.5 = (f32[2048]{0:T(1024)S(1)}, f32[2048]{0:T(1024)}, u32[]{:S(2)}) copy-start(f32[2048]{0:T(1024)} %param.18) | copy-start | bytes 24580
  143.4 5.7 %copy-start.2 = (s32[960,8]{0,1:T(8,128)S(1)}, s32[960,8]{0,1:T(8,128)}, u32[]{:S(2)}) copy-start(s32[960,8]{0,1:T(8,128)} %param.22) | copy-start | bytes 92164
  143.4 11.7 %copy-start.3 = (f32[960,8]{0,1:T(8,128)S(1)}, f32[960,8]{0,1:T(8,128)}, u32[]{:S(2)}) copy-start(f32[960,8]{0,1:T(8,128)} %param.23) | copy-start | bytes 92164
  143.4 51.7 %all-to-all-start = ((bf16[4,240,2048]{2,1,0:T(8,128)(2,1)}), bf16[4,240,2048]{2,1,0:T(8,128)(2,1)}, u32[]{:S(2)}, u32[]{:S(2)}) async-start(bf16[4,240,2048]{2,1,0:T(8,128)(2,1)} %stack.2), calls=%async_computation.1 | async-start | bytes 7864320 | tf_op jit(solution)/shard_map/all_to_all | solution.py:118
  149.1 154.2 %reduce-scatter.5.cloned.1.call-start = ((), (), s32[]{:S(2)}) async-start(), calls=%async_computation.4 | async-start | bytes 9830400 | tf_op jit(solution)/shard_map/reduce_scatter | solution.py:132
Sparse Core Ops, SparseCore 0:
  53.6 85.1 reduce-scatter.2
  222.7 80.5 reduce-scatter.4
